TPU v7x, 32 devices: a whole 2x2x4 slice. The times are simulated.
32 devices in a mesh: sector: 8 (over y, x, core), sub: 4 (over z).
Axes of the slice: x: 2, y: 2, z: 4, core: 2. Of those that a mesh axis runs over, the one named last changes fastest.
Arguments:
- dual_load: float32 [8, 4, 2, 512, 256], P('sector', 'sub'), may hold values from -50 to 50
- flexibility: bfloat16 [8, 4, 2048, 2048], P('sector', 'sub'), may hold values from -10 to 10, as said below
- face_order: int32 [8, 4, 2048], P('sector', 'sub'), may hold values from 0 to 2047, each once within a row
- corner_index: int32 [8, 4, 32], P('sector', 'sub'), may hold values from 0 to 2047, as said below
- coarse_inverse: float32 [256, 256], replicated, may hold values from -10 to 10, as said below
Outputs:
- multiplier: float32 [8, 4, 2, 512, 256], P('sector', 'sub')
- residual: float32 [8, 4, 2, 512, 256], P('sector', 'sub')
Inputs may be any that keep to these rules, and one draw needn't show every extreme that they name: `flexibility`: a block of sizes of order one with a dominant diagonal; each subdomain's matrix is symmetric positive definite. `corner_index`: entries within one subdomain are distinct. `face_order`: each subdomain's row names every face slot once. `coarse_inverse`: symmetric positive definite with a dominant diagonal.
All inputs are finite; a program needn't handle non-finite values.
Results may differ from a plain program's by a relative error of at most 0.0087.
The roundings to bfloat16 on the way count: a program that leaves them out, or rounds other values in their place, can miss the bound.
Values may be sent and summed in bfloat16 or wider, within the bound.
No kernel may reach another device: no remote copies, remote signals or barrier semaphores. Data moves between devices by JAX's collectives and lax.ppermute only.
A program may use at most 128 MiB of HBM per device.

v0:
```python
import jax
import jax.numpy as jnp
from jax import lax
from jax.sharding import PartitionSpec as P

ITERS = 2


def passed_along(x, axis, by):
    count = lax.axis_size(axis)
    pairs = [(i, i + by) for i in range(count) if 0 <= i + by < count]
    return lax.ppermute(x, axis, pairs)


def from_behind(value, axis, steps):
    count = lax.axis_size(axis)
    pairs = [(source, (source + steps) % count) for source in range(count)]
    return lax.ppermute(value, axis, pairs)


def squares(residual):
    return lax.psum(jnp.sum(residual * residual, axis=(0, 1, 2, 3)), ("sector", "sub"))


def inner_sum(left, right):
    return jnp.sum(left * right, axis=(0, 1, 2, 3))


def shards(dual_load, flexibility, face_order, corner_index, coarse_inverse):
    slot_order = face_order[0, 0]
    corners = corner_index[0, 0]
    corner_count = corners.shape[0]
    slot_count = slot_order.shape[0]
    own_place = (
        jnp.zeros((slot_count,), jnp.int32)
        .at[slot_order]
        .set(jnp.arange(slot_count, dtype=jnp.int32))
    )
    matrix = flexibility[0, 0]
    face_width = slot_order.shape[0] // 4
    cases = dual_load.shape[-1]
    sub_count = lax.axis_size("sub")
    multiplier = jnp.zeros_like(dual_load)
    residual = dual_load
    direction = dual_load
    norm_now = squares(residual)
    for iteration in range(ITERS):
        rounded = direction[0, 0].astype(jnp.bfloat16)
        lower_sub = passed_along(rounded[0], "sub", 1)
        previous = from_behind(rounded[1], "sector", 1)
        face_stack = jnp.concatenate([-lower_sub, rounded[0], -previous, rounded[1]], axis=0)
        partial_value = jnp.take(face_stack, corners, axis=0).astype(jnp.float32)
        sector_total = lax.psum(partial_value.astype(jnp.bfloat16), "sub").astype(jnp.float32)
        sector_id = lax.axis_index("sector")
        everything = lax.all_gather(sector_total, "sector", axis=0, tiled=True)
        inverse_rows = lax.dynamic_slice_in_dim(
            coarse_inverse, sector_id * corner_count, corner_count, 0
        )
        coarse = jnp.dot(
            inverse_rows,
            everything,
            precision=lax.Precision.HIGHEST,
            preferred_element_type=jnp.float32,
        )
        coarse = coarse / sub_count
        correction = jnp.zeros((4 * face_width, cases), jnp.float32).at[corners].add(coarse)
        own_faces = jnp.take(face_stack, own_place, axis=0)
        own_product = jnp.dot(matrix, own_faces, preferred_element_type=jnp.float32)
        product = jnp.take(own_product, slot_order, axis=0) + correction
        outgoing_sub = product[:face_width]
        outgoing_cycle = product[2 * face_width : 3 * face_width]
        upper_next = passed_along(outgoing_sub.astype(jnp.bfloat16), "sub", -1)
        cycle_next = from_behind(outgoing_cycle.astype(jnp.bfloat16), "sector", -1)
        own_sub = product[face_width : 2 * face_width]
        own_cycle = product[3 * face_width :]
        jump_pair = jnp.stack(
            [own_sub - upper_next.astype(jnp.float32), own_cycle - cycle_next.astype(jnp.float32)],
            axis=0,
        )
        image = jump_pair[None, None]
        curvature = lax.psum(inner_sum(direction, image), ("sector", "sub"))
        alpha = norm_now / curvature
        multiplier = multiplier + alpha * direction
        residual = residual - alpha * image
        if iteration + 1 < ITERS:
            norm_next = squares(residual)
            direction = residual + norm_next / norm_now * direction
            norm_now = norm_next
    return (multiplier, residual)


def solution(mesh):
    return jax.shard_map(
        shards,
        mesh=mesh,
        in_specs=(
            P("sector", "sub", None, None, None),
            P("sector", "sub", None, None),
            P("sector", "sub", None),
            P("sector", "sub", None),
            P(),
        ),
        out_specs=(P("sector", "sub", None, None, None), P("sector", "sub", None, None, None)),
        check_vma=False,
    )
```

profile of v0, /device:TPU:10, one launch (start us, length us, event | category | flops | bytes accessed | tf_op | source)
XLA Modules:
  0.0 280.6 jit_solution(3341148262424951663)
XLA Ops:
  2.0 3.5 %collective-permute-start = (bf16[512,256]{1,0:T(8,128)(2,1)S(1)}, bf16[512,256]{1,0:T(8,128)(2,1)S(1)}, u32[]{:S(2)}, u32[]{:S(2)}) collective-permute-start(bf16[512,256]{1,0:T(8,128)(2,1)S(1)} %get-tuple-element.29), channel_id=1, source_target_pairs={{0,1},{1,2},{2,3},{4,5},{5,6},{6,7},{8,9},{9,10},{10,11},{12,13},{... | collective-permute-start | bytes 786440 | tf_op jit(solution)/shard_map/ppermute | solution.py:12
  5.7 8.0 %scatter_custom_fusion = s32[2048]{0:T(1024)S(1)} fusion(s32[2048]{0:T(1024)S(1)} %bitcast.66, s32[2048]{0:T(1024)S(1)} %iota.3, s32[]{:T(128)} %constant.11.clone.1), kind=kCustom, calls=%fused_computation.70 | custom fusion | bytes 8196 | tf_op jit(solution)/shard_map/scatter | solution.py:37
  14.6 7.5 %gather_fusion = bf16[2048,256]{1,0:T(8,128)(2,1)S(1)} fusion(bf16[2048,256]{1,0:T(8,128)(2,1)S(1)} %pad_maximum_fusion, s32[2048]{0:T(1024)S(1)} %fusion.33), kind=kCustom, calls=%fused_computation.clone | custom fusion | bytes 2105344 | tf_op jit(solution)/shard_map/jit(_take)/gather | solution.py:67
  22.2 14.2 %psum.43 = bf16[32,256]{1,0:T(8,128)(2,1)S(1)} all-reduce(bf16[32,256]{1,0:T(8,128)(2,1)S(1)} %broadcast_select_fusion.3), channel_id=1, replica_groups=mesh['sector'=8,'sub'=4] {'sub'}, use_global_device_ids=true, to_apply=%region_3.7 | all-reduce | flops 8192 | bytes 32768 | tf_op jit(solution)/shard_map/psum | solution.py:53
  36.5 9.3 %all_gather.6 = f32[256,256]{1,0:T(8,128)S(1)} all-gather(f32[32,256]{1,0:T(8,128)S(1)} %convert_element_type.35), channel_id=1, replica_groups=mesh['sector'=8,'sub'=4] {'sector'}, dimensions={0}, use_global_device_ids=true | all-gather | bytes 294912 | tf_op jit(solution)/shard_map/all_gather | solution.py:55
  45.8 7.5 %fusion.4 = f32[2048,256]{0,1:T(8,128)} fusion(bf16[1,1,2048,2048]{3,2,1,0:T(8,128)(2,1)} %param.12, bf16[2048,256]{1,0:T(8,128)(2,1)S(1)} %gather_fusion, pred[2048]{0:T(1024)(128)(4,1)S(1)} %compare_and_fusion.1), kind=kOutput, calls=%fused_computation.13 | convolution fusion | flops 2148007936 | bytes 11536384 | tf_op jit(solution)/shard_map/dot_general | solution.py:68
  53.3 1.9 copy.9
  55.2 8.6 %gather_fusion.1 = f32[2048,256]{1,0:T(8,128)} fusion(f32[2048,256]{1,0:T(8,128)S(1)} %copy.9, s32[2048]{0:T(1024)S(1)} %fusion.34), kind=kCustom, calls=%fused_computation.1.clone | custom fusion | bytes 4202496 | tf_op jit(solution)/shard_map/jit(_take)/gather | solution.py:69
  63.8 1.9 broadcast_select_fusion.1
  67.7 5.4 %collective-permute-start.2 = (bf16[512,256]{1,0:T(8,128)(2,1)S(1)}, bf16[512,256]{1,0:T(8,128)(2,1)S(1)}, u32[]{:S(2)}, u32[]{:S(2)}) collective-permute-start(bf16[512,256]{1,0:T(8,128)(2,1)S(1)} %get-tuple-element.25), channel_id=1, source_target_pairs={{1,0},{2,1},{3,2},{5,4},{6,5},{7,6},{9,8},{10,9},{11,10},{13,12},{... | collective-permute-start | bytes 786440 | tf_op jit(solution)/shard_map/ppermute | solution.py:12
  73.3 5.8 %collective-permute-done.2 = bf16[512,256]{1,0:T(8,128)(2,1)S(1)} collective-permute-done((bf16[512,256]{1,0:T(8,128)(2,1)S(1)}, bf16[512,256]{1,0:T(8,128)(2,1)S(1)}, u32[]{:S(2)}, u32[]{:S(2)}) %collective-permute-start.2) | collective-permute-done | bytes 262176 | tf_op jit(solution)/shard_map/ppermute | solution.py:12
  80.6 40.9 %all-reduce = (f32[256]{0:T(256)S(1)}, f32[256]{0:T(256)S(1)}) all-reduce(f32[256]{0:T(256)S(1)} %get-tuple-element.6, f32[256]{0:T(256)S(1)} %get-tuple-element.4), channel_id=1, replica_groups=mesh['sector'=8,'sub'=4] {'sector','sub'}, use_global_device_ids=true, to_apply=%region_1.0 | all-reduce | flops 512 | bytes 4096 | tf_op jit(solution)/shard_map/psum | solution.py:22
  121.7 39.4 %psum.45 = f32[256]{0:T(256)S(1)} all-reduce(f32[256]{0:T(256)S(1)} %multiply_reduce_fusion), channel_id=1, replica_groups=mesh['sector'=8,'sub'=4] {'sector','sub'}, use_global_device_ids=true, to_apply=%region_8.12 | all-reduce | flops 256 | bytes 2048 | tf_op jit(solution)/shard_map/psum | solution.py:22
  161.3 2.6 collective-permute-start.4
  164.0 5.6 %collective-permute-done.4 = bf16[512,256]{1,0:T(8,128)(2,1)S(1)} collective-permute-done((bf16[512,256]{1,0:T(8,128)(2,1)S(1)}, bf16[512,256]{1,0:T(8,128)(2,1)S(1)}, u32[]{:S(2)}, u32[]{:S(2)}) %collective-permute-start.4) | collective-permute-done | bytes 262176 | tf_op jit(solution)/shard_map/ppermute | solution.py:12
  170.5 7.5 %gather_fusion.3 = bf16[2048,256]{1,0:T(8,128)(2,1)S(1)} fusion(bf16[2048,256]{1,0:T(8,128)(2,1)S(1)} %pad_maximum_fusion.1, s32[2048]{0:T(1024)S(1)} %fusion.33), kind=kCustom, calls=%fused_computation.3.clone | custom fusion | bytes 2105344 | tf_op jit(solution)/shard_map/jit(_take)/gather | solution.py:67
  178.1 14.9 %psum.46 = bf16[32,256]{1,0:T(8,128)(2,1)S(1)} all-reduce(bf16[32,256]{1,0:T(8,128)(2,1)S(1)} %broadcast_select_fusion.2), channel_id=1, replica_groups=mesh['sector'=8,'sub'=4] {'sub'}, use_global_device_ids=true, to_apply=%region_9.13 | all-reduce | flops 8192 | bytes 32768 | tf_op jit(solution)/shard_map/psum | solution.py:53
  193.0 9.3 %all_gather.7 = f32[256,256]{1,0:T(8,128)S(1)} all-gather(f32[32,256]{1,0:T(8,128)S(1)} %convert_element_type.39), channel_id=1, replica_groups=mesh['sector'=8,'sub'=4] {'sector'}, dimensions={0}, use_global_device_ids=true | all-gather | bytes 294912 | tf_op jit(solution)/shard_map/all_gather | solution.py:55
  202.6 7.5 %fusion.7 = f32[2048,256]{0,1:T(8,128)} fusion(bf16[1,1,2048,2048]{3,2,1,0:T(8,128)(2,1)} %param.12, bf16[2048,256]{1,0:T(8,128)(2,1)S(1)} %gather_fusion.3, pred[2048]{0:T(1024)(128)(4,1)S(1)} %compare_and_fusion.1), kind=kOutput, calls=%fused_computation.14 | convolution fusion | flops 2148007936 | bytes 11536384 | tf_op jit(solution)/shard_map/dot_general | solution.py:68
  212.0 8.6 %gather_fusion.4 = f32[2048,256]{1,0:T(8,128)} fusion(f32[2048,256]{1,0:T(8,128)S(1)} %copy.10, s32[2048]{0:T(1024)S(1)} %fusion.34), kind=kCustom, calls=%fused_computation.4.clone | custom fusion | bytes 4202496 | tf_op jit(solution)/shard_map/jit(_take)/gather | solution.py:69
  220.6 1.9 broadcast_select_fusion
  224.3 6.1 %collective-permute-start.6 = (bf16[512,256]{1,0:T(8,128)(2,1)S(1)}, bf16[512,256]{1,0:T(8,128)(2,1)S(1)}, u32[]{:S(2)}, u32[]{:S(2)}) collective-permute-start(bf16[512,256]{1,0:T(8,128)(2,1)S(1)} %get-tuple-element.23), channel_id=1, source_target_pairs={{1,0},{2,1},{3,2},{5,4},{6,5},{7,6},{9,8},{10,9},{11,10},{13,12},{... | collective-permute-start | bytes 786440 | tf_op jit(solution)/shard_map/ppermute | solution.py:12
  230.7 5.7 %collective-permute-done.6 = bf16[512,256]{1,0:T(8,128)(2,1)S(1)} collective-permute-done((bf16[512,256]{1,0:T(8,128)(2,1)S(1)}, bf16[512,256]{1,0:T(8,128)(2,1)S(1)}, u32[]{:S(2)}, u32[]{:S(2)}) %collective-permute-start.6) | collective-permute-done | bytes 262176 | tf_op jit(solution)/shard_map/ppermute | solution.py:12
  237.9 41.0 %psum.47 = f32[256]{0:T(256)S(1)} all-reduce(f32[256]{0:T(256)S(1)} %fusion.14), channel_id=1, replica_groups=mesh['sector'=8,'sub'=4] {'sector','sub'}, use_global_device_ids=true, to_apply=%region_12.16 | all-reduce | flops 256 | bytes 2048 | tf_op jit(solution)/shard_map/psum | solution.py:81
  (77 shorter events, 14.6 us)
Async XLA Ops:
  0.6 65.1 %copy-start = (f32[256,256]{1,0:T(8,128)S(1)}, f32[256,256]{1,0:T(8,128)}, u32[]{:S(2)}) copy-start(f32[256,256]{1,0:T(8,128)} %param.15) | copy-start | bytes 786436
  0.6 4.9 %copy-start.11 = (s32[1,1,32]{2,1,0:T(1,128)S(1)}, s32[1,1,32]{2,1,0:T(1,128)}, u32[]{:S(2)}) copy-start(s32[1,1,32]{2,1,0:T(1,128)} %param.14) | copy-start | bytes 388
  0.7 5.0 %copy-start.10 = (s32[1,1,2048]{2,1,0:T(1,128)S(1)}, s32[1,1,2048]{2,1,0:T(1,128)}, u32[]{:S(2)}) copy-start(s32[1,1,2048]{2,1,0:T(1,128)} %param.13) | copy-start | bytes 24580
  2.0 11.8 %collective-permute-start = (bf16[512,256]{1,0:T(8,128)(2,1)S(1)}, bf16[512,256]{1,0:T(8,128)(2,1)S(1)}, u32[]{:S(2)}, u32[]{:S(2)}) collective-permute-start(bf16[512,256]{1,0:T(8,128)(2,1)S(1)} %get-tuple-element.29), channel_id=1, source_target_pairs={{0,1},{1,2},{2,3},{4,5},{5,6},{6,7},{8,9},{9,10},{10,11},{12,13},{... | collective-permute-start | bytes 786440 | tf_op jit(solution)/shard_map/ppermute | solution.py:12
  5.5 8.4 %collective-permute-start.1 = (bf16[512,256]{1,0:T(8,128)(2,1)S(1)}, bf16[512,256]{1,0:T(8,128)(2,1)S(1)}, u32[]{:S(2)}, u32[]{:S(2)}) collective-permute-start(bf16[512,256]{1,0:T(8,128)(2,1)S(1)} %get-tuple-element.30), channel_id=1, source_target_pairs={{0,4},{4,8},{8,12},{12,16},{16,20},{20,24},{24,28},{28,0},{1,5},{5... | collective-permute-start | bytes 786440 | tf_op jit(solution)/shard_map/ppermute | solution.py:18
  67.7 12.6 %copy-start.1 = (f32[1,1,2,512,256]{4,3,2,1,0:T(8,128)S(1)}, f32[1,1,2,512,256]{4,3,2,1,0:T(8,128)}, u32[]{:S(2)}) copy-start(f32[1,1,2,512,256]{4,3,2,1,0:T(8,128)} %param.11) | copy-start | bytes 3145732
  67.7 11.5 %collective-permute-start.2 = (bf16[512,256]{1,0:T(8,128)(2,1)S(1)}, bf16[512,256]{1,0:T(8,128)(2,1)S(1)}, u32[]{:S(2)}, u32[]{:S(2)}) collective-permute-start(bf16[512,256]{1,0:T(8,128)(2,1)S(1)} %get-tuple-element.25), channel_id=1, source_target_pairs={{1,0},{2,1},{3,2},{5,4},{6,5},{7,6},{9,8},{10,9},{11,10},{13,12},{... | collective-permute-start | bytes 786440 | tf_op jit(solution)/shard_map/ppermute | solution.py:12
  73.1 6.1 %collective-permute-start.3 = (bf16[512,256]{1,0:T(8,128)(2,1)S(1)}, bf16[512,256]{1,0:T(8,128)(2,1)S(1)}, u32[]{:S(2)}, u32[]{:S(2)}) collective-permute-start(bf16[512,256]{1,0:T(8,128)(2,1)S(1)} %get-tuple-element.26), channel_id=1, source_target_pairs={{0,28},{4,0},{8,4},{12,8},{16,12},{20,16},{24,20},{28,24},{1,29},{... | collective-permute-start | bytes 786440 | tf_op jit(solution)/shard_map/ppermute | solution.py:18
  80.3 41.2 %copy-start.2 = (f32[1,1,1,512,256]{4,3,2,1,0:T(8,128)S(1)}, f32[1,1,1,512,256]{4,3,2,1,0:T(8,128)}, u32[]{:S(2)}) copy-start(f32[1,1,1,512,256]{4,3,2,1,0:T(8,128)} %get-tuple-element.14) | copy-start | bytes 1572868
  80.3 41.2 %copy-start.5 = (f32[1,1,1,512,256]{4,3,2,1,0:T(8,128)S(1)}, f32[1,1,1,512,256]{4,3,2,1,0:T(8,128)}, u32[]{:S(2)}) copy-start(f32[1,1,1,512,256]{4,3,2,1,0:T(8,128)} %get-tuple-element.21) | copy-start | bytes 1572868
  161.3 8.3 %collective-permute-start.4 = (bf16[512,256]{1,0:T(8,128)(2,1)S(1)}, bf16[512,256]{1,0:T(8,128)(2,1)S(1)}, u32[]{:S(2)}, u32[]{:S(2)}) collective-permute-start(bf16[512,256]{1,0:T(8,128)(2,1)S(1)} %get-tuple-element.27), channel_id=1, source_target_pairs={{0,1},{1,2},{2,3},{4,5},{5,6},{6,7},{8,9},{9,10},{10,11},{12,13},{... | collective-permute-start | bytes 786440 | tf_op jit(solution)/shard_map/ppermute | solution.py:12
  163.9 5.8 %collective-permute-start.5 = (bf16[512,256]{1,0:T(8,128)(2,1)S(1)}, bf16[512,256]{1,0:T(8,128)(2,1)S(1)}, u32[]{:S(2)}, u32[]{:S(2)}) collective-permute-start(bf16[512,256]{1,0:T(8,128)(2,1)S(1)} %get-tuple-element.28), channel_id=1, source_target_pairs={{0,4},{4,8},{8,12},{12,16},{16,20},{20,24},{24,28},{28,0},{1,5},{5... | collective-permute-start | bytes 786440 | tf_op jit(solution)/shard_map/ppermute | solution.py:18
  224.2 13.4 %copy-start.3 = (f32[1,1,1,512,256]{4,3,2,1,0:T(8,128)S(1)}, f32[1,1,1,512,256]{4,3,2,1,0:T(8,128)}, u32[]{:S(2)}) copy-start(f32[1,1,1,512,256]{4,3,2,1,0:T(8,128)} %get-tuple-element.14) | copy-start | bytes 1572868
  224.2 13.4 %copy-start.6 = (f32[1,1,1,512,256]{4,3,2,1,0:T(8,128)S(1)}, f32[1,1,1,512,256]{4,3,2,1,0:T(8,128)}, u32[]{:S(2)}) copy-start(f32[1,1,1,512,256]{4,3,2,1,0:T(8,128)} %get-tuple-element.21) | copy-start | bytes 1572868
  224.3 12.2 %collective-permute-start.6 = (bf16[512,256]{1,0:T(8,128)(2,1)S(1)}, bf16[512,256]{1,0:T(8,128)(2,1)S(1)}, u32[]{:S(2)}, u32[]{:S(2)}) collective-permute-start(bf16[512,256]{1,0:T(8,128)(2,1)S(1)} %get-tuple-element.23), channel_id=1, source_target_pairs={{1,0},{2,1},{3,2},{5,4},{6,5},{7,6},{9,8},{10,9},{11,10},{13,12},{... | collective-permute-start | bytes 786440 | tf_op jit(solution)/shard_map/ppermute | solution.py:12
  230.4 6.1 %collective-permute-start.7 = (bf16[512,256]{1,0:T(8,128)(2,1)S(1)}, bf16[512,256]{1,0:T(8,128)(2,1)S(1)}, u32[]{:S(2)}, u32[]{:S(2)}) collective-permute-start(bf16[512,256]{1,0:T(8,128)(2,1)S(1)} %get-tuple-element.24), channel_id=1, source_target_pairs={{0,28},{4,0},{8,4},{12,8},{16,12},{20,16},{24,20},{28,24},{1,29},{... | collective-permute-start | bytes 786440 | tf_op jit(solution)/shard_map/ppermute | solution.py:18
  237.6 41.3 %copy-start.4 = (f32[1,1,1,512,256]{4,3,2,1,0:T(8,128)S(1)}, f32[1,1,1,512,256]{4,3,2,1,0:T(8,128)}, u32[]{:S(2)}) copy-start(f32[1,1,1,512,256]{4,3,2,1,0:T(8,128)} %get-tuple-element.14) | copy-start | bytes 1572868
  237.6 41.3 %copy-start.7 = (f32[1,1,1,512,256]{4,3,2,1,0:T(8,128)S(1)}, f32[1,1,1,512,256]{4,3,2,1,0:T(8,128)}, u32[]{:S(2)}) copy-start(f32[1,1,1,512,256]{4,3,2,1,0:T(8,128)} %get-tuple-element.21) | copy-start | bytes 1572868
  237.6 41.3 %copy-start.8 = (f32[1,1,1,512,256]{4,3,2,1,0:T(8,128)S(1)}, f32[1,1,1,512,256]{4,3,2,1,0:T(8,128)}, u32[]{:S(2)}) copy-start(f32[1,1,1,512,256]{4,3,2,1,0:T(8,128)} %get-tuple-element.9) | copy-start | bytes 1572868
  237.6 41.3 %copy-start.9 = (f32[1,1,1,512,256]{4,3,2,1,0:T(8,128)S(1)}, f32[1,1,1,512,256]{4,3,2,1,0:T(8,128)}, u32[]{:S(2)}) copy-start(f32[1,1,1,512,256]{4,3,2,1,0:T(8,128)} %get-tuple-element.20) | copy-start | bytes 1572868
where the time goes:
time: 281 us
  blocking collectives  169 us (60%)
  local copies, waits for them, and re-layouts  45.5 us (16%)
  starting transfers between devices  18.3 us (7%)
  waiting for transfers between devices  17.3 us (6%)
  matrix products  15.5 us (6%)
  other arithmetic  13.8 us (5%)
    psum x2, blocking collectives, squares(): lax.psum(jnp.sum(residual * residual, axis=(0, 1, 2, 3)), ('sector', 'sub'))  80.3 us
    psum x1, blocking collectives, shards(): curvature = lax.psum(inner_sum(direction, image), ('sector', 'sub'))  41 us
    psum x2, blocking collectives, shards(): lax.psum(partial_value.astype(jnp.bfloat16), 'sub').astype(jnp.float32)  29.2 us
    all_gather x2, blocking collectives, shards(): everything = lax.all_gather(sector_total, 'sector', axis=0, tiled=True)  18.6 us
    ppermute x4, starting transfers between devices, passed_along(): return lax.ppermute(x, axis, pairs)  17.6 us
    ppermute x4, waiting for transfers between devices, passed_along(): return lax.ppermute(x, axis, pairs)  17.2 us
    gather x2, local copies, waits for them, and re-layouts, shards(): product = jnp.take(own_product, slot_order, axis=0) + correction  17.1 us
    dot_general x2, matrix products, shards(): own_product = jnp.dot(matrix, own_faces, preferred_element_type=jnp.float32)  15 us
  transfers between devices with their start and end apart: 8, of which 4 were waited for; matrix products, arithmetic and copies ran while one was open for 3% of the time, Pallas kernels for 0%

commit v1 on v0

--- a/solution.py
+++ b/solution.py
@@ -52,7 +52,19 @@
         partial_value = jnp.take(face_stack, corners, axis=0).astype(jnp.float32)
         sector_total = lax.psum(partial_value.astype(jnp.bfloat16), "sub").astype(jnp.float32)
         sector_id = lax.axis_index("sector")
-        everything = lax.all_gather(sector_total, "sector", axis=0, tiled=True)
+        n_now, now = (jax.lax.psum(1, axis_name="sector"), jax.lax.axis_index("sector"))
+        everything, mixed_arr = (sector_total, 1)
+        while mixed_arr < n_now:
+            so_far_all = []
+            it = 0
+            while it < n_now:
+                so_far_all.append((it, it ^ mixed_arr))
+                it += 1
+            arr_now = jax.lax.ppermute(everything, axis_name="sector", perm=so_far_all)
+            far_arr = jnp.concatenate([everything, arr_now], axis=0)
+            arr_out = jnp.concatenate([arr_now, everything], axis=0)
+            everything = jnp.where(now & mixed_arr == 0, far_arr, arr_out)
+            mixed_arr = 2 * mixed_arr
         inverse_rows = lax.dynamic_slice_in_dim(
             coarse_inverse, sector_id * corner_count, corner_count, 0
         )

time: 281 us -> 272 us (0.968)
  blocking collectives: 169 us -> 152 us
  starting transfers between devices: 18.3 us -> 22.8 us
    all_gather x2 -> x0, blocking collectives: 18.6 us -> none  [shards(): everything = lax.all_gather(sector_total, 'sector', axis=0, tiled=True)]
    ppermute x0 -> x6, starting transfers between devices: none -> 5.37 us  [shards(): arr_now = jax.lax.ppermute(everything, axis_name='sector', perm=so_far_all)]
    ppermute x0 -> x6, waiting for transfers between devices: none -> 4.07 us  [shards(): arr_now = jax.lax.ppermute(everything, axis_name='sector', perm=so_far_all)]
  transfers between devices with their start and end apart: 8 -> 14, of which waited for: 4 -> 6; matrix products, arithmetic and copies ran while one was open for 3% -> 23% of each run, Pallas kernels for 0% -> 0%
where the time goes in v1:
time: 272 us
  blocking collectives  152 us (56%)
  local copies, waits for them, and re-layouts  45.6 us (17%)
  starting transfers between devices  22.8 us (8%)
  waiting for transfers between devices  19.5 us (7%)
  matrix products  15.5 us (6%)
  other arithmetic  14.8 us (5%)
    psum x2, blocking collectives, squares(): lax.psum(jnp.sum(residual * residual, axis=(0, 1, 2, 3)), ('sector', 'sub'))  81.3 us
    psum x1, blocking collectives, shards(): curvature = lax.psum(inner_sum(direction, image), ('sector', 'sub'))  41.8 us
    psum x2, blocking collectives, shards(): lax.psum(partial_value.astype(jnp.bfloat16), 'sub').astype(jnp.float32)  29.2 us
    gather x2, local copies, waits for them, and re-layouts, shards(): product = jnp.take(own_product, slot_order, axis=0) + correction  17.2 us
    ppermute x4, starting transfers between devices, passed_along(): return lax.ppermute(x, axis, pairs)  17 us
    ppermute x4, waiting for transfers between devices, passed_along(): return lax.ppermute(x, axis, pairs)  15.4 us
    dot_general x2, matrix products, shards(): own_product = jnp.dot(matrix, own_faces, preferred_element_type=jnp.float32)  15 us
    gather x2, local copies, waits for them, and re-layouts, shards(): own_faces = jnp.take(face_stack, own_place, axis=0)  15 us
  transfers between devices with their start and end apart: 14, of which 6 were waited for; matrix products, arithmetic and copies ran while one was open for 23% of the time, Pallas kernels for 0%

profile of v1, /device:TPU:10, one launch (start us, length us, event | category | flops | bytes accessed | tf_op | source)
XLA Modules:
  0.0 271.7 jit_solution(6558979093125296109)
XLA Ops:
  2.0 3.5 %collective-permute-start = (bf16[512,256]{1,0:T(8,128)(2,1)S(1)}, bf16[512,256]{1,0:T(8,128)(2,1)S(1)}, u32[]{:S(2)}, u32[]{:S(2)}) collective-permute-start(bf16[512,256]{1,0:T(8,128)(2,1)S(1)} %get-tuple-element.29), channel_id=1, source_target_pairs={{0,1},{1,2},{2,3},{4,5},{5,6},{6,7},{8,9},{9,10},{10,11},{12,13},{... | collective-permute-start | bytes 786440 | tf_op jit(solution)/shard_map/ppermute | solution.py:12
  5.7 8.0 %scatter_custom_fusion = s32[2048]{0:T(1024)S(1)} fusion(s32[2048]{0:T(1024)S(1)} %bitcast.64, s32[2048]{0:T(1024)S(1)} %iota.3, s32[]{:T(128)} %constant.6.clone.1), kind=kCustom, calls=%fused_computation.88 | custom fusion | bytes 8196 | tf_op jit(solution)/shard_map/scatter | solution.py:37
  14.7 14.2 %psum.43 = bf16[32,256]{1,0:T(8,128)(2,1)S(1)} all-reduce(bf16[32,256]{1,0:T(8,128)(2,1)S(1)} %broadcast_select_fusion.3), channel_id=1, replica_groups=mesh['sector'=8,'sub'=4] {'sub'}, use_global_device_ids=true, to_apply=%region_3.7 | all-reduce | flops 8192 | bytes 32768 | tf_op jit(solution)/shard_map/psum | solution.py:53
  29.1 7.5 %gather_fusion = bf16[2048,256]{1,0:T(8,128)(2,1)S(1)} fusion(bf16[2048,256]{1,0:T(8,128)(2,1)S(1)} %pad_maximum_fusion, s32[2048]{0:T(1024)S(1)} %fusion.45), kind=kCustom, calls=%fused_computation.clone | custom fusion | bytes 2105344 | tf_op jit(solution)/shard_map/jit(_take)/gather | solution.py:79
  37.2 7.5 %fusion.4 = f32[2048,256]{0,1:T(8,128)} fusion(bf16[1,1,2048,2048]{3,2,1,0:T(8,128)(2,1)} %param.12, bf16[2048,256]{1,0:T(8,128)(2,1)S(1)} %gather_fusion, pred[2048]{0:T(1024)(128)(4,1)S(1)} %compare_and_fusion.1), kind=kOutput, calls=%fused_computation.13 | convolution fusion | flops 2148007936 | bytes 11536384 | tf_op jit(solution)/shard_map/dot_general | solution.py:80
  46.6 8.6 %gather_fusion.1 = f32[2048,256]{1,0:T(8,128)} fusion(f32[2048,256]{1,0:T(8,128)S(1)} %copy.9, s32[2048]{0:T(1024)S(1)} %fusion.46), kind=kCustom, calls=%fused_computation.1.clone | custom fusion | bytes 4202496 | tf_op jit(solution)/shard_map/jit(_take)/gather | solution.py:81
  56.8 1.9 broadcast_select_fusion.1
  58.8 2.1 collective-permute-done.4
  62.9 5.4 %collective-permute-start.5 = (bf16[512,256]{1,0:T(8,128)(2,1)S(1)}, bf16[512,256]{1,0:T(8,128)(2,1)S(1)}, u32[]{:S(2)}, u32[]{:S(2)}) collective-permute-start(bf16[512,256]{1,0:T(8,128)(2,1)S(1)} %get-tuple-element.25), channel_id=1, source_target_pairs={{1,0},{2,1},{3,2},{5,4},{6,5},{7,6},{9,8},{10,9},{11,10},{13,12},{... | collective-permute-start | bytes 786440 | tf_op jit(solution)/shard_map/ppermute | solution.py:12
  68.5 4.8 %collective-permute-done.5 = bf16[512,256]{1,0:T(8,128)(2,1)S(1)} collective-permute-done((bf16[512,256]{1,0:T(8,128)(2,1)S(1)}, bf16[512,256]{1,0:T(8,128)(2,1)S(1)}, u32[]{:S(2)}, u32[]{:S(2)}) %collective-permute-start.5) | collective-permute-done | bytes 262176 | tf_op jit(solution)/shard_map/ppermute | solution.py:12
  74.7 41.9 %all-reduce = (f32[256]{0:T(256)S(1)}, f32[256]{0:T(256)S(1)}) all-reduce(f32[256]{0:T(256)S(1)} %get-tuple-element.6, f32[256]{0:T(256)S(1)} %get-tuple-element.4), channel_id=1, replica_groups=mesh['sector'=8,'sub'=4] {'sector','sub'}, use_global_device_ids=true, to_apply=%region_1.0 | all-reduce | flops 512 | bytes 4096 | tf_op jit(solution)/shard_map/psum | solution.py:22
  116.8 39.4 %psum.45 = f32[256]{0:T(256)S(1)} all-reduce(f32[256]{0:T(256)S(1)} %multiply_reduce_fusion), channel_id=1, replica_groups=mesh['sector'=8,'sub'=4] {'sector','sub'}, use_global_device_ids=true, to_apply=%region_8.12 | all-reduce | flops 256 | bytes 2048 | tf_op jit(solution)/shard_map/psum | solution.py:22
  156.5 2.6 collective-permute-start.7
  159.1 5.6 %collective-permute-done.7 = bf16[512,256]{1,0:T(8,128)(2,1)S(1)} collective-permute-done((bf16[512,256]{1,0:T(8,128)(2,1)S(1)}, bf16[512,256]{1,0:T(8,128)(2,1)S(1)}, u32[]{:S(2)}, u32[]{:S(2)}) %collective-permute-start.7) | collective-permute-done | bytes 262176 | tf_op jit(solution)/shard_map/ppermute | solution.py:12
  165.7 15.0 %psum.46 = bf16[32,256]{1,0:T(8,128)(2,1)S(1)} all-reduce(bf16[32,256]{1,0:T(8,128)(2,1)S(1)} %broadcast_select_fusion.2), channel_id=1, replica_groups=mesh['sector'=8,'sub'=4] {'sub'}, use_global_device_ids=true, to_apply=%region_9.13 | all-reduce | flops 8192 | bytes 32768 | tf_op jit(solution)/shard_map/psum | solution.py:53
  180.8 7.5 %gather_fusion.3 = bf16[2048,256]{1,0:T(8,128)(2,1)S(1)} fusion(bf16[2048,256]{1,0:T(8,128)(2,1)S(1)} %pad_maximum_fusion.1, s32[2048]{0:T(1024)S(1)} %fusion.45), kind=kCustom, calls=%fused_computation.3.clone | custom fusion | bytes 2105344 | tf_op jit(solution)/shard_map/jit(_take)/gather | solution.py:79
  189.0 7.5 %fusion.7 = f32[2048,256]{0,1:T(8,128)} fusion(bf16[1,1,2048,2048]{3,2,1,0:T(8,128)(2,1)} %param.12, bf16[2048,256]{1,0:T(8,128)(2,1)S(1)} %gather_fusion.3, pred[2048]{0:T(1024)(128)(4,1)} %copy-done.17), kind=kOutput, calls=%fused_computation.14 | convolution fusion | flops 2148007936 | bytes 11536384 | tf_op jit(solution)/shard_map/dot_general | solution.py:80
  198.4 8.6 %gather_fusion.4 = f32[2048,256]{1,0:T(8,128)} fusion(f32[2048,256]{1,0:T(8,128)S(1)} %copy.10, s32[2048]{0:T(1024)S(1)} %fusion.46), kind=kCustom, calls=%fused_computation.4.clone | custom fusion | bytes 4202496 | tf_op jit(solution)/shard_map/jit(_take)/gather | solution.py:81
  208.0 2.3 collective-permute-start.11
  210.3 1.9 broadcast_select_fusion
  212.2 1.9 collective-permute-done.11
  216.2 5.5 %collective-permute-start.12 = (bf16[512,256]{1,0:T(8,128)(2,1)S(1)}, bf16[512,256]{1,0:T(8,128)(2,1)S(1)}, u32[]{:S(2)}, u32[]{:S(2)}) collective-permute-start(bf16[512,256]{1,0:T(8,128)(2,1)S(1)} %get-tuple-element.23), channel_id=1, source_target_pairs={{1,0},{2,1},{3,2},{5,4},{6,5},{7,6},{9,8},{10,9},{11,10},{13,12},{... | collective-permute-start | bytes 786440 | tf_op jit(solution)/shard_map/ppermute | solution.py:12
  221.8 4.9 %collective-permute-done.12 = bf16[512,256]{1,0:T(8,128)(2,1)S(1)} collective-permute-done((bf16[512,256]{1,0:T(8,128)(2,1)S(1)}, bf16[512,256]{1,0:T(8,128)(2,1)S(1)}, u32[]{:S(2)}, u32[]{:S(2)}) %collective-permute-start.12) | collective-permute-done | bytes 262176 | tf_op jit(solution)/shard_map/ppermute | solution.py:12
  228.2 41.8 %psum.47 = f32[256]{0:T(256)S(1)} all-reduce(f32[256]{0:T(256)S(1)} %fusion.14), channel_id=1, replica_groups=mesh['sector'=8,'sub'=4] {'sector','sub'}, use_global_device_ids=true, to_apply=%region_12.16 | all-reduce | flops 256 | bytes 2048 | tf_op jit(solution)/shard_map/psum | solution.py:93
  (105 shorter events, 20.3 us)
Async XLA Ops:
  0.6 60.3 %copy-start = (f32[256,256]{1,0:T(8,128)S(1)}, f32[256,256]{1,0:T(8,128)}, u32[]{:S(2)}) copy-start(f32[256,256]{1,0:T(8,128)} %param.15) | copy-start | bytes 786436
  2.0 11.8 %collective-permute-start = (bf16[512,256]{1,0:T(8,128)(2,1)S(1)}, bf16[512,256]{1,0:T(8,128)(2,1)S(1)}, u32[]{:S(2)}, u32[]{:S(2)}) collective-permute-start(bf16[512,256]{1,0:T(8,128)(2,1)S(1)} %get-tuple-element.29), channel_id=1, source_target_pairs={{0,1},{1,2},{2,3},{4,5},{5,6},{6,7},{8,9},{9,10},{10,11},{12,13},{... | collective-permute-start | bytes 786440 | tf_op jit(solution)/shard_map/ppermute | solution.py:12
  5.5 8.3 %collective-permute-start.1 = (bf16[512,256]{1,0:T(8,128)(2,1)S(1)}, bf16[512,256]{1,0:T(8,128)(2,1)S(1)}, u32[]{:S(2)}, u32[]{:S(2)}) collective-permute-start(bf16[512,256]{1,0:T(8,128)(2,1)S(1)} %get-tuple-element.30), channel_id=1, source_target_pairs={{0,4},{4,8},{8,12},{12,16},{16,20},{20,24},{24,28},{28,0},{1,5},{5... | collective-permute-start | bytes 786440 | tf_op jit(solution)/shard_map/ppermute | solution.py:18
  13.8 23.4 %copy-start.17 = (pred[2048]{0:T(1024)(128)(4,1)}, pred[2048]{0:T(1024)(128)(4,1)S(1)}, u32[]{:S(2)}) copy-start(pred[2048]{0:T(1024)(128)(4,1)S(1)} %compare_and_fusion.1) | copy-start | bytes 6148
  28.9 7.6 %collective-permute-start.2 = (f32[32,256]{1,0:T(8,128)S(1)}, f32[32,256]{1,0:T(8,128)S(1)}, u32[]{:S(2)}, u32[]{:S(2)}) collective-permute-start(f32[32,256]{1,0:T(8,128)S(1)} %convert_element_type.35), channel_id=1, source_target_pairs={{0,4},{4,0},{8,12},{12,8},{16,20},{20,16},{24,28},{28,24},{1,5},{5... | collective-permute-start | bytes 98312 | tf_op jit(solution)/shard_map/ppermute | solution.py:63
  29.0 32.1 %copy-start.15 = (s32[32]{0:T(128)}, s32[32]{0:T(128)S(1)}, u32[]{:S(2)}) copy-start(s32[32]{0:T(128)S(1)} %fusion.49) | copy-start | bytes 388
  36.6 18.6 %collective-permute-start.3 = (f32[64,256]{1,0:T(8,128)S(1)}, f32[64,256]{1,0:T(8,128)S(1)}, u32[]{:S(2)}, u32[]{:S(2)}) collective-permute-start(f32[64,256]{1,0:T(8,128)S(1)} %maximum_select_fusion.6), channel_id=1, source_target_pairs={{0,8},{4,12},{8,0},{12,4},{16,24},{20,28},{24,16},{28,20},{1,9},{5... | collective-permute-start | bytes 196616 | tf_op jit(solution)/shard_map/ppermute | solution.py:63
  55.2 5.6 %collective-permute-start.4 = (f32[128,256]{1,0:T(8,128)S(1)}, f32[128,256]{1,0:T(8,128)S(1)}, u32[]{:S(2)}, u32[]{:S(2)}) collective-permute-start(f32[128,256]{1,0:T(8,128)S(1)} %maximum_select_fusion.4), channel_id=1, source_target_pairs={{0,16},{4,20},{8,24},{12,28},{16,0},{20,4},{24,8},{28,12},{1,17},{... | collective-permute-start | bytes 393224 | tf_op jit(solution)/shard_map/ppermute | solution.py:63
  62.9 10.4 %collective-permute-start.5 = (bf16[512,256]{1,0:T(8,128)(2,1)S(1)}, bf16[512,256]{1,0:T(8,128)(2,1)S(1)}, u32[]{:S(2)}, u32[]{:S(2)}) collective-permute-start(bf16[512,256]{1,0:T(8,128)(2,1)S(1)} %get-tuple-element.25), channel_id=1, source_target_pairs={{1,0},{2,1},{3,2},{5,4},{6,5},{7,6},{9,8},{10,9},{11,10},{13,12},{... | collective-permute-start | bytes 786440 | tf_op jit(solution)/shard_map/ppermute | solution.py:12
  68.3 5.0 %collective-permute-start.6 = (bf16[512,256]{1,0:T(8,128)(2,1)S(1)}, bf16[512,256]{1,0:T(8,128)(2,1)S(1)}, u32[]{:S(2)}, u32[]{:S(2)}) collective-permute-start(bf16[512,256]{1,0:T(8,128)(2,1)S(1)} %get-tuple-element.26), channel_id=1, source_target_pairs={{0,28},{4,0},{8,4},{12,8},{16,12},{20,16},{24,20},{28,24},{1,29},{... | collective-permute-start | bytes 786440 | tf_op jit(solution)/shard_map/ppermute | solution.py:18
  74.4 42.2 %copy-start.2 = (f32[1,1,1,512,256]{4,3,2,1,0:T(8,128)S(1)}, f32[1,1,1,512,256]{4,3,2,1,0:T(8,128)}, u32[]{:S(2)}) copy-start(f32[1,1,1,512,256]{4,3,2,1,0:T(8,128)} %get-tuple-element.14) | copy-start | bytes 1572868
  74.4 42.2 %copy-start.5 = (f32[1,1,1,512,256]{4,3,2,1,0:T(8,128)S(1)}, f32[1,1,1,512,256]{4,3,2,1,0:T(8,128)}, u32[]{:S(2)}) copy-start(f32[1,1,1,512,256]{4,3,2,1,0:T(8,128)} %get-tuple-element.21) | copy-start | bytes 1572868
  156.5 8.3 %collective-permute-start.7 = (bf16[512,256]{1,0:T(8,128)(2,1)S(1)}, bf16[512,256]{1,0:T(8,128)(2,1)S(1)}, u32[]{:S(2)}, u32[]{:S(2)}) collective-permute-start(bf16[512,256]{1,0:T(8,128)(2,1)S(1)} %get-tuple-element.27), channel_id=1, source_target_pairs={{0,1},{1,2},{2,3},{4,5},{5,6},{6,7},{8,9},{9,10},{10,11},{12,13},{... | collective-permute-start | bytes 786440 | tf_op jit(solution)/shard_map/ppermute | solution.py:12
  159.0 5.8 %collective-permute-start.8 = (bf16[512,256]{1,0:T(8,128)(2,1)S(1)}, bf16[512,256]{1,0:T(8,128)(2,1)S(1)}, u32[]{:S(2)}, u32[]{:S(2)}) collective-permute-start(bf16[512,256]{1,0:T(8,128)(2,1)S(1)} %get-tuple-element.28), channel_id=1, source_target_pairs={{0,4},{4,8},{8,12},{12,16},{16,20},{20,24},{24,28},{28,0},{1,5},{5... | collective-permute-start | bytes 786440 | tf_op jit(solution)/shard_map/ppermute | solution.py:18
  180.7 7.6 %collective-permute-start.9 = (f32[32,256]{1,0:T(8,128)S(1)}, f32[32,256]{1,0:T(8,128)S(1)}, u32[]{:S(2)}, u32[]{:S(2)}) collective-permute-start(f32[32,256]{1,0:T(8,128)S(1)} %convert_element_type.39), channel_id=1, source_target_pairs={{0,4},{4,0},{8,12},{12,8},{16,20},{20,16},{24,28},{28,24},{1,5},{5... | collective-permute-start | bytes 98312 | tf_op jit(solution)/shard_map/ppermute | solution.py:63
  188.3 18.7 %collective-permute-start.10 = (f32[64,256]{1,0:T(8,128)S(1)}, f32[64,256]{1,0:T(8,128)}, u32[]{:S(2)}, u32[]{:S(2)}) collective-permute-start(f32[64,256]{1,0:T(8,128)S(1)} %maximum_select_fusion.7), channel_id=1, source_target_pairs={{0,8},{4,12},{8,0},{12,4},{16,24},{20,28},{24,16},{28,20},{1,9},{5... | collective-permute-start | bytes 196616 | tf_op jit(solution)/shard_map/ppermute | solution.py:63
  208.0 6.2 %collective-permute-start.11 = (f32[128,256]{1,0:T(8,128)S(1)}, f32[128,256]{1,0:T(8,128)S(1)}, u32[]{:S(2)}, u32[]{:S(2)}) collective-permute-start(f32[128,256]{1,0:T(8,128)S(1)} %maximum_select_fusion.5), channel_id=1, source_target_pairs={{0,16},{4,20},{8,24},{12,28},{16,0},{20,4},{24,8},{28,12},{1,17},{... | collective-permute-start | bytes 393224 | tf_op jit(solution)/shard_map/ppermute | solution.py:63
  216.2 10.6 %collective-permute-start.12 = (bf16[512,256]{1,0:T(8,128)(2,1)S(1)}, bf16[512,256]{1,0:T(8,128)(2,1)S(1)}, u32[]{:S(2)}, u32[]{:S(2)}) collective-permute-start(bf16[512,256]{1,0:T(8,128)(2,1)S(1)} %get-tuple-element.23), channel_id=1, source_target_pairs={{1,0},{2,1},{3,2},{5,4},{6,5},{7,6},{9,8},{10,9},{11,10},{13,12},{... | collective-permute-start | bytes 786440 | tf_op jit(solution)/shard_map/ppermute | solution.py:12
  221.7 5.1 %collective-permute-start.13 = (bf16[512,256]{1,0:T(8,128)(2,1)S(1)}, bf16[512,256]{1,0:T(8,128)(2,1)S(1)}, u32[]{:S(2)}, u32[]{:S(2)}) collective-permute-start(bf16[512,256]{1,0:T(8,128)(2,1)S(1)} %get-tuple-element.24), channel_id=1, source_target_pairs={{0,28},{4,0},{8,4},{12,8},{16,12},{20,16},{24,20},{28,24},{1,29},{... | collective-permute-start | bytes 786440 | tf_op jit(solution)/shard_map/ppermute | solution.py:18
  227.9 42.1 %copy-start.14 = (f32[256]{0:T(256)S(1)}, f32[256]{0:T(256)}, u32[]{:S(2)}) copy-start(f32[256]{0:T(256)} %copy-done.13) | copy-start | bytes 3076
  227.9 42.1 %copy-start.4 = (f32[1,1,1,512,256]{4,3,2,1,0:T(8,128)S(1)}, f32[1,1,1,512,256]{4,3,2,1,0:T(8,128)}, u32[]{:S(2)}) copy-start(f32[1,1,1,512,256]{4,3,2,1,0:T(8,128)} %get-tuple-element.14) | copy-start | bytes 1572868
  227.9 42.1 %copy-start.7 = (f32[1,1,1,512,256]{4,3,2,1,0:T(8,128)S(1)}, f32[1,1,1,512,256]{4,3,2,1,0:T(8,128)}, u32[]{:S(2)}) copy-start(f32[1,1,1,512,256]{4,3,2,1,0:T(8,128)} %get-tuple-element.21) | copy-start | bytes 1572868
  227.9 42.1 %copy-start.8 = (f32[1,1,1,512,256]{4,3,2,1,0:T(8,128)S(1)}, f32[1,1,1,512,256]{4,3,2,1,0:T(8,128)}, u32[]{:S(2)}) copy-start(f32[1,1,1,512,256]{4,3,2,1,0:T(8,128)} %get-tuple-element.9) | copy-start | bytes 1572868
  227.9 42.2 %copy-start.9 = (f32[1,1,1,512,256]{4,3,2,1,0:T(8,128)S(1)}, f32[1,1,1,512,256]{4,3,2,1,0:T(8,128)}, u32[]{:S(2)}) copy-start(f32[1,1,1,512,256]{4,3,2,1,0:T(8,128)} %get-tuple-element.20) | copy-start | bytes 1572868
  (9 other events, 80.3 us)
